TPU v7x, 256 devices: a whole 4x4x8 slice. The times are simulated.
256 devices in a mesh: row: 8 (over z), col: 32 (over x, y, core).
Axes of the slice: x: 4, y: 4, z: 8, core: 2. Of those that a mesh axis runs over, the one named last changes fastest.
Arguments:
- tile_values: float32 [8, 32, 128, 128, 128], P('row', 'col')
- tile_coords: int32 [8, 32, 128, 2], P('row', 'col'), may hold values from 0 to 271, as said below
- tile_count: int32 [8, 32], P('row', 'col'), may hold values from 16 to 128, as said below
- objective: float32 [262144], P('col')
- lower: float32 [262144], P('col'), may hold values from -2 to -0.2
- upper: float32 [262144], P('col'), may hold values from 0.2 to 2
- rhs: float32 [278528], P('row')
- primal_start: float32 [262144], P('col'), may hold values from -4 to 4
- dual_start: float32 [278528], P('row'), may hold values from 0 to 1
- step_size: float32 [1], replicated, may hold values from 0.02 to 0.06
Outputs:
- primal_solution: float32 [262144], P('col')
- dual_solution: float32 [278528], P('row')
Inputs may be any that keep to these rules, and one draw needn't show every extreme that they name: `tile_coords`: coordinates are local: block rows 0 to 271, block columns 0 to 63, also in unused slots. Devices whose col index is congruent to their row index modulo the size of row hold one period: their block rows are (col index // size of row) * 64 plus 0 to 63. All other devices hold only linking block rows, 256 to 271. Every block row and every block column of A is met by some used slot. `tile_count`: period devices use all slots; other devices use 16 to 64 slots.
All inputs are finite; a program needn't handle non-finite values.
Results may differ from a plain program's by a relative error of at most 0.00012.
Values sent between devices are 32-bit elements; how exact they have to be, the bound alone decides.
No kernel may reach another device: no remote copies, remote signals or barrier semaphores. Data moves between devices by JAX's collectives and lax.ppermute only.
A program may use at most 64 MiB of HBM per device.

v0:
```python
import jax
import jax.numpy as jnp
from jax import lax
from jax.sharding import PartitionSpec as P

RUIZ = 2
ITERS = 2
EPSILON = 1e-06
HIGHEST = lax.Precision.HIGHEST


def local(
    tile_values,
    tile_coords,
    tile_count,
    objective,
    lower,
    upper,
    rhs,
    primal_start,
    dual_start,
    step_size,
):
    tile_width = tile_values.shape[-1]
    slot_count = tile_values.shape[2]
    matrix = tile_values.reshape(slot_count, tile_width, tile_width)
    coords = tile_coords.reshape(slot_count, 2)
    block_rows = coords[:, 0]
    block_cols = coords[:, 1]
    row_blocks = rhs.shape[0] // tile_width
    col_blocks = objective.shape[0] // tile_width
    in_use = (jnp.arange(slot_count, dtype=jnp.int32) < tile_count.reshape(())).astype(jnp.float32)
    row_onehot = (jnp.arange(row_blocks, dtype=jnp.int32)[:, None] == block_rows[None, :]).astype(
        jnp.float32
    ) * in_use[None, :]
    col_onehot = (jnp.arange(col_blocks, dtype=jnp.int32)[:, None] == block_cols[None, :]).astype(
        jnp.float32
    ) * in_use[None, :]
    magnitude = jnp.abs(matrix) * in_use[:, None, None]
    row_scale = jnp.ones((row_blocks, tile_width), jnp.float32)
    col_scale = jnp.ones((col_blocks, tile_width), jnp.float32)
    for sweep in range(RUIZ):
        col_pieces = jnp.take(col_scale, block_cols, axis=0)
        row_pieces = jnp.take(row_scale, block_rows, axis=0)
        row_local = jnp.max(magnitude * col_pieces[:, None, :], axis=2)
        col_local = jnp.max(magnitude * row_pieces[:, :, None], axis=1)
        row_peak = jnp.zeros((row_blocks, tile_width), jnp.float32).at[block_rows].max(row_local)
        col_peak = jnp.zeros((col_blocks, tile_width), jnp.float32).at[block_cols].max(col_local)
        peak_target = row_peak
        peak_joined = lax.pmax(peak_target, "col")
        row_peak = peak_joined
        col_peak = lax.pmax(col_peak, "row")
        row_scale = row_scale / jnp.sqrt(row_scale * row_peak + EPSILON)
        col_scale = col_scale / jnp.sqrt(col_scale * col_peak + EPSILON)
    cost = col_scale * objective.reshape(col_blocks, tile_width)
    bound = row_scale * rhs.reshape(row_blocks, tile_width)
    low_scaled = lower.reshape(col_blocks, tile_width) / col_scale
    high_scaled = upper.reshape(col_blocks, tile_width) / col_scale
    primal = primal_start.reshape(col_blocks, tile_width) / col_scale
    dual = dual_start.reshape(row_blocks, tile_width) / row_scale
    cost_square = jnp.sum(cost * cost)
    bound_square = jnp.sum(bound * bound)
    cost_total = lax.psum(cost_square, "col")
    bound_total = lax.psum(bound_square, "row")
    weight = jnp.sqrt(cost_total + EPSILON) / jnp.sqrt(bound_total + EPSILON)
    primal_step = step_size[0] / weight
    dual_step = step_size[0] * weight
    for iteration in range(ITERS):
        pieces = jnp.take(row_scale * dual, block_rows, axis=0)
        products = jnp.einsum("tij,ti->tj", matrix, pieces, precision=HIGHEST)
        image = lax.psum(jnp.dot(col_onehot, products, precision=HIGHEST), "row")
        moved = jnp.clip(primal - primal_step * (cost - col_scale * image), low_scaled, high_scaled)
        extra = 2.0 * moved - primal
        forward_pieces = jnp.take(col_scale * extra, block_cols, axis=0)
        forward_products = jnp.einsum("tij,tj->ti", matrix, forward_pieces, precision=HIGHEST)
        partial_rows = jnp.dot(row_onehot, forward_products, precision=HIGHEST)
        total = lax.psum(partial_rows, "col")
        dual = jnp.maximum(dual + dual_step * (bound - row_scale * total), 0.0)
        primal = moved
    return ((col_scale * primal).reshape(-1), (row_scale * dual).reshape(-1))


def solution(mesh):
    placed = (
        P("row", "col", None, None, None),
        P("row", "col", None, None),
        P("row", "col"),
        P("col"),
        P("col"),
        P("col"),
        P("row"),
        P("col"),
        P("row"),
        P(),
    )
    return jax.shard_map(
        local, mesh=mesh, in_specs=placed, out_specs=(P("col"), P("row")), check_vma=False
    )
```

profile of v0, /device:TPU:1, one launch (start us, length us, event | category | flops | bytes accessed | tf_op | source)
XLA Modules:
  0.0 609.2 jit_solution(8344150141682839794)
XLA Ops:
  7.2 0.0 all-reduce.10.cloned.1.call-start
  7.2 0.8 compare_and_fusion
  8.0 0.8 slice_bitcast_fusion
  9.4 0.6 gather_fusion
  10.1 0.1 broadcast_select_fusion.7
  10.2 5.7 multiply_reduce_fusion.3
  15.9 1.0 scatter_custom_fusion
  16.9 26.6 %pmax.28 = f32[64,128]{1,0:T(8,128)S(1)} all-reduce(f32[64,128]{1,0:T(8,128)S(1)} %scatter_custom_fusion), channel_id=1, replica_groups=mesh['row'=8,'col'=32] {'row'}, use_global_device_ids=true, to_apply=%region_2.4 | all-reduce | flops 8192 | bytes 65536 | tf_op jit(solution)/shard_map/pmax | solution.py:52
  43.5 0.6 gather_fusion.3
  44.2 0.6 gather_fusion.1
  44.8 0.1 broadcast_select_fusion.6
  44.9 7.3 %multiply_reduce_fusion = (f32[128,128]{1,0:T(8,128)S(1)}, f32[128,128]{1,0:T(8,128)S(1)}) fusion(f32[1,1,128,128,128]{4,3,2,1,0:T(8,128)} %param.14, f32[128,128]{1,0:T(8,128)S(1)} %get-tuple-element.30, f32[128]{0:T(128)S(1)} %compare_convert_fusion, f32[128,128]{1,0:T(8,128)S(1)} %get-tuple-element.29), kind=kLoop, calls=%fused_computation.22 | loop fusion | flops 12550144 | bytes 8651264 | tf_op jit(solution)/shard_map/reduce_max | solution.py:45
  52.2 1.6 scatter_custom_fusion.3
  53.8 1.6 scatter_custom_fusion.1
  55.5 0.0 all-reduce.10.cloned.1.call-update
  55.5 0.0 all-reduce.6.cloned.1.call-start
  56.2 116.2 %all-reduce.10.cloned.1.call-done = (f32[272,128]{1,0:T(8,128)}, f32[272,128]{1,0:T(8,128)}) async-done(((f32[272,128]{1,0:T(8,128)}, f32[272,128]{1,0:T(8,128)}), (f32[272,128]{1,0:T(8,128)}, f32[272,128]{1,0:T(8,128)})) %all-reduce.10.cloned.1.call-update) | async-done | bytes 278544 | tf_op jit(solution)/shard_map/pmax | solution.py:50
  172.4 1.6 multiply_reduce_fusion.4
  174.0 0.6 gather_fusion.4
  174.7 0.6 gather_fusion.2
  175.3 0.1 broadcast_select_fusion.3
  175.5 9.4 %fusion.6 = f32[128,1,128]{2,1,0:T(1,128)S(1)} fusion(f32[128,128,1]{1,2,0:T(1,128)S(1)} %bitcast.129, f32[1,1,128,128,128]{4,3,2,1,0:T(8,128)} %param.14), kind=kOutput, calls=%fused_computation.18 | convolution fusion | flops 25165824 | bytes 8519680 | tf_op jit(solution)/shard_map/tij,ti->tj/dot_general | solution.py:70
  184.9 0.2 fusion.27
  185.1 24.6 %all-reduce.1 = (f32[64,128]{1,0:T(8,128)S(1)}, f32[]{:T(128)}) all-reduce(f32[64,128]{1,0:T(8,128)S(1)} %fusion.27, f32[]{:T(128)} %get-tuple-element.12), channel_id=1, replica_groups=mesh['row'=8,'col'=32] {'row'}, use_global_device_ids=true, to_apply=%region_16.19 | all-reduce | flops 8193 | bytes 65544 | tf_op jit(solution)/shard_map/psum | solution.py:71
  210.3 5.7 multiply_reduce_fusion.1
  216.0 1.0 scatter_custom_fusion.2
  217.1 20.4 %pmax.30 = f32[64,128]{1,0:T(8,128)S(1)} all-reduce(f32[64,128]{1,0:T(8,128)S(1)} %scatter_custom_fusion.2), channel_id=1, replica_groups=mesh['row'=8,'col'=32] {'row'}, use_global_device_ids=true, to_apply=%region_8.11 | all-reduce | flops 8192 | bytes 65536 | tf_op jit(solution)/shard_map/pmax | solution.py:52
  237.4 0.6 multiply_reduce_fusion.5
  238.0 77.9 %psum.42 = f32[]{:T(128)} all-reduce(f32[]{:T(128)} %get-tuple-element.10), channel_id=1, replica_groups=mesh['row'=8,'col'=32] {'col'}, use_global_device_ids=true, to_apply=%region_10.13 | all-reduce | flops 1 | bytes 8 | tf_op jit(solution)/shard_map/psum | solution.py:63
  316.8 0.6 gather_fusion.5
  317.4 0.1 broadcast_select_fusion.2
  317.5 15.4 %fusion.4 = f32[128,1,128]{2,1,0:T(1,128)S(1)} fusion(f32[128,128,1]{1,2,0:T(1,128)S(1)} %bitcast.128, f32[1,1,128,128,128]{4,3,2,1,0:T(8,128)} %param.14), kind=kOutput, calls=%fused_computation.16 | convolution fusion | flops 25165824 | bytes 8519680 | tf_op jit(solution)/shard_map/tij,tj->ti/dot_general | solution.py:75
  332.9 0.9 fusion.11
  333.8 0.0 all-reduce.8.cloned.1.call-start
  333.9 103.0 %all-reduce.6.cloned.1.call-done = f32[272,128]{1,0:T(8,128)} async-done(((f32[272,128]{1,0:T(8,128)}), f32[272,128]{1,0:T(8,128)}) %all-reduce.6.cloned.1.call-update) | async-done | bytes 139280 | tf_op jit(solution)/shard_map/psum | solution.py:77
  436.9 1.0 fusion.13
  437.8 0.6 gather_fusion.6
  438.5 0.1 broadcast_select_fusion.1
  438.6 9.4 %fusion.2 = f32[128,1,128]{2,1,0:T(1,128)S(1)} fusion(f32[128,128,1]{1,2,0:T(1,128)S(1)} %bitcast.124, f32[1,1,128,128,128]{4,3,2,1,0:T(8,128)} %param.14), kind=kOutput, calls=%fused_computation.14 | convolution fusion | flops 25165824 | bytes 8519680 | tf_op jit(solution)/shard_map/tij,ti->tj/dot_general | solution.py:70
  448.0 0.2 fusion.25
  448.2 23.4 %psum.46 = f32[64,128]{1,0:T(8,128)S(1)} all-reduce(f32[64,128]{1,0:T(8,128)S(1)} %fusion.25), channel_id=1, replica_groups=mesh['row'=8,'col'=32] {'row'}, use_global_device_ids=true, to_apply=%region_18.21 | all-reduce | flops 8192 | bytes 65536 | tf_op jit(solution)/shard_map/psum | solution.py:71
  471.5 0.6 subtract_multiply_fusion
  472.2 0.6 gather_fusion.7
  472.8 0.1 broadcast_select_fusion
  472.9 15.4 %fusion = f32[128,1,128]{2,1,0:T(1,128)S(1)} fusion(f32[128,128,1]{1,2,0:T(1,128)S(1)} %bitcast.126, f32[1,1,128,128,128]{4,3,2,1,0:T(8,128)} %param.14), kind=kOutput, calls=%fused_computation.12 | convolution fusion | flops 25165824 | bytes 8519680 | tf_op jit(solution)/shard_map/tij,tj->ti/dot_general | solution.py:75
  488.3 0.9 fusion.9
  489.3 111.7 %all-reduce.8.cloned.1.call-done = f32[272,128]{1,0:T(8,128)} async-done(((f32[272,128]{1,0:T(8,128)}), f32[272,128]{1,0:T(8,128)}) %all-reduce.8.cloned.1.call-update) | async-done | bytes 139280 | tf_op jit(solution)/shard_map/psum | solution.py:77
  601.0 1.6 multiply_bitcast_fusion
  (24 shorter events, 0.2 us)
Async XLA Ops:
  7.2 165.2 %all-reduce.10.cloned.1.call-start = ((), (), s32[]{:S(2)}) async-start(), calls=%async_computation.2 | async-start | bytes 557056 | tf_op jit(solution)/shard_map/pmax | solution.py:50
  10.2 162.2 %copy-start = (f32[34816]{0:T(1024)S(1)}, f32[34816]{0:T(1024)}, u32[]{:S(2)}) copy-start(f32[34816]{0:T(1024)} %param.20) | copy-start | bytes 417796
  10.2 163.8 %copy-start.1 = (f32[34816]{0:T(1024)S(1)}, f32[34816]{0:T(1024)}, u32[]{:S(2)}) copy-start(f32[34816]{0:T(1024)} %param.22) | copy-start | bytes 417796
  55.5 381.4 %all-reduce.6.cloned.1.call-start = ((), (), s32[]{:S(2)}) async-start(), calls=%async_computation | async-start | bytes 278528 | tf_op jit(solution)/shard_map/psum | solution.py:77
  175.4 62.0 %copy-start.3 = (f32[8192]{0:T(1024)S(1)}, f32[8192]{0:T(1024)}, u32[]{:S(2)}) copy-start(f32[8192]{0:T(1024)} %param.17) | copy-start | bytes 98308
  175.4 141.3 %copy-start.4 = (f32[8192]{0:T(1024)S(1)}, f32[8192]{0:T(1024)}, u32[]{:S(2)}) copy-start(f32[8192]{0:T(1024)} %param.19) | copy-start | bytes 98308
  175.4 141.3 %copy-start.5 = (f32[8192]{0:T(1024)S(1)}, f32[8192]{0:T(1024)}, u32[]{:S(2)}) copy-start(f32[8192]{0:T(1024)} %param.18) | copy-start | bytes 98308
  175.5 141.3 %copy-start.6 = (f32[8192]{0:T(1024)S(1)}, f32[8192]{0:T(1024)}, u32[]{:S(2)}) copy-start(f32[8192]{0:T(1024)} %param.21) | copy-start | bytes 98308
  333.8 267.1 %all-reduce.8.cloned.1.call-start = ((), (), s32[]{:S(2)}) async-start(), calls=%async_computation.1 | async-start | bytes 278528 | tf_op jit(solution)/shard_map/psum | solution.py:77
  438.6 162.4 %copy-start.2 = (f32[272,128]{1,0:T(8,128)S(1)}, f32[272,128]{1,0:T(8,128)}, u32[]{:S(2)}) copy-start(f32[272,128]{1,0:T(8,128)} %all-reduce.6.cloned.1.call-done) | copy-start | bytes 417796
Sparse Core Ops, SparseCore 0:
  55.6 116.7 all-reduce.9
  334.0 102.8 all-reduce.5
  489.4 111.5 all-reduce.7
where the time goes:
time: 610 us; the launch traced here: 609 us
  waiting for transfers between devices  331 us (54%)
  blocking collectives  173 us (28%)
  matrix products  51.8 us (8%)
  other arithmetic  31.6 us (5%)
  between operations  16.7 us (3%)
    psum x2, waiting for transfers between devices, local(): total = lax.psum(partial_rows, 'col')  215 us
    pmax x1, waiting for transfers between devices, local(): peak_joined = lax.pmax(peak_target, 'col')  116 us
    psum x1, blocking collectives, local(): cost_total = lax.psum(cost_square, 'col')  77.9 us
    psum x2, blocking collectives, local(): image = lax.psum(jnp.dot(col_onehot, products, precision=HIGHEST), 'row')  47.9 us
    pmax x2, blocking collectives, local(): col_peak = lax.pmax(col_peak, 'row')  46.9 us
    dot_general x2, matrix products, local(): jnp.einsum('tij,tj->ti', matrix, forward_pieces, precision=HIGHEST)  30.8 us
    dot_general x2, matrix products, local(): products = jnp.einsum('tij,ti->tj', matrix, pieces, precision=HIGHEST)  18.8 us
  transfers between devices with their start and end apart: 3, of which 3 were waited for; matrix products, arithmetic and copies ran while one was open for 0% of the time, Pallas kernels for 0%

commit v1 on v0

--- a/solution.py
+++ b/solution.py
@@ -7,6 +7,15 @@
 ITERS = 2
 EPSILON = 1e-06
 HIGHEST = lax.Precision.HIGHEST
+
+
+def sum_by_hops(x, axis):
+    devices = lax.axis_size(axis)
+    total, far = (x, 1)
+    while far < devices:
+        total = total + lax.ppermute(total, axis, [(i, i ^ far) for i in range(devices)])
+        far = 2 * far
+    return total
 
 
 def local(
@@ -74,7 +83,7 @@
         forward_pieces = jnp.take(col_scale * extra, block_cols, axis=0)
         forward_products = jnp.einsum("tij,tj->ti", matrix, forward_pieces, precision=HIGHEST)
         partial_rows = jnp.dot(row_onehot, forward_products, precision=HIGHEST)
-        total = lax.psum(partial_rows, "col")
+        total = sum_by_hops(partial_rows, "col")
         dual = jnp.maximum(dual + dual_step * (bound - row_scale * total), 0.0)
         primal = moved
     return ((col_scale * primal).reshape(-1), (row_scale * dual).reshape(-1))

time: 610 us -> 449 us (0.74)
  waiting for transfers between devices: 331 us -> 157 us
  starting transfers between devices: 0.12 us -> 21.8 us
  blocking collectives: 173 us -> 164 us
    psum x2 -> x0, waiting for transfers between devices: 215 us -> none  [local(): total = lax.psum(partial_rows, 'col')]
    ppermute x0 -> x10, waiting for transfers between devices: none -> 41.1 us  [sum_by_hops(): lax.ppermute(total, axis, [(i, i ^ far) for i in range(devices)])]
    ppermute x0 -> x10, starting transfers between devices: none -> 21.8 us  [sum_by_hops(): lax.ppermute(total, axis, [(i, i ^ far) for i in range(devices)])]
    psum x1, blocking collectives: 77.9 us -> 70.8 us  [local(): cost_total = lax.psum(cost_square, 'col')]
  transfers between devices with their start and end apart: 3 -> 11, of which waited for: 3 -> 11; matrix products, arithmetic and copies ran while one was open for 0% -> 0% of each run, Pallas kernels for 0% -> 0%
where the time goes in v1:
time: 449 us; the launch traced here: 446 us
  blocking collectives  164 us (37%)
  waiting for transfers between devices  157 us (35%)
  matrix products  50.5 us (11%)
  other arithmetic  29.9 us (7%)
  starting transfers between devices  21.8 us (5%)
  between operations  17.1 us (4%)
  local copies, waits for them, and re-layouts  5.21 us (1%)
    pmax x1, waiting for transfers between devices, local(): peak_joined = lax.pmax(peak_target, 'col')  116 us
    psum x1, blocking collectives, local(): cost_total = lax.psum(cost_square, 'col')  70.8 us
    pmax x2, blocking collectives, local(): col_peak = lax.pmax(col_peak, 'row')  49.8 us
    psum x2, blocking collectives, local(): image = lax.psum(jnp.dot(col_onehot, products, precision=HIGHEST), 'row')  43.4 us
    ppermute x10, waiting for transfers between devices, sum_by_hops(): lax.ppermute(total, axis, [(i, i ^ far) for i in range(devices)])  41.1 us
    dot_general x2, matrix products, local(): jnp.einsum('tij,tj->ti', matrix, forward_pieces, precision=HIGHEST)  30.8 us
    ppermute x10, starting transfers between devices, sum_by_hops(): lax.ppermute(total, axis, [(i, i ^ far) for i in range(devices)])  21.8 us
    dot_general x2, matrix products, local(): products = jnp.einsum('tij,ti->tj', matrix, pieces, precision=HIGHEST)  18.8 us
  transfers between devices with their start and end apart: 11, of which 11 were waited for; matrix products, arithmetic and copies ran while one was open for 0% of the time, Pallas kernels for 0%

profile of v1, /device:TPU:1, one launch (start us, length us, event | category | flops | bytes accessed | tf_op | source)
XLA Modules:
  0.0 445.8 jit_solution(11676373317948062848)
XLA Ops:
  7.2 0.8 slice_bitcast_fusion
  8.0 0.8 compare_and_fusion
  9.4 0.6 gather_fusion
  10.2 5.7 %multiply_reduce_fusion.3 = f32[128,128]{1,0:T(8,128)S(1)} fusion(f32[1,1,128,128,128]{4,3,2,1,0:T(8,128)} %param.14, f32[128,128]{1,0:T(8,128)S(1)} %broadcast_select_fusion.7, f32[128]{0:T(128)S(1)} %compare_convert_fusion), kind=kLoop, calls=%fused_computation.25 | loop fusion | flops 8372224 | bytes 8520192 | tf_op jit(solution)/shard_map/reduce_max | solution.py:55
  15.9 1.0 scatter_custom_fusion
  17.0 26.6 %pmax.28 = f32[64,128]{1,0:T(8,128)S(1)} all-reduce(f32[64,128]{1,0:T(8,128)S(1)} %scatter_custom_fusion), channel_id=1, replica_groups=mesh['row'=8,'col'=32] {'row'}, use_global_device_ids=true, to_apply=%region_2.4 | all-reduce | flops 8192 | bytes 65536 | tf_op jit(solution)/shard_map/pmax | solution.py:61
  43.6 0.6 gather_fusion.1
  44.2 0.6 gather_fusion.3
  45.0 7.3 %multiply_reduce_fusion = (f32[128,128]{1,0:T(8,128)S(1)}, f32[128,128]{1,0:T(8,128)S(1)}) fusion(f32[1,1,128,128,128]{4,3,2,1,0:T(8,128)} %param.14, f32[128,128]{1,0:T(8,128)S(1)} %get-tuple-element.30, f32[128]{0:T(128)S(1)} %compare_convert_fusion, f32[128,128]{1,0:T(8,128)S(1)} %get-tuple-element.29), kind=kLoop, calls=%fused_computation.22 | loop fusion | flops 12550144 | bytes 8651264 | tf_op jit(solution)/shard_map/reduce_max | solution.py:54
  52.2 1.6 scatter_custom_fusion.3
  53.9 1.6 scatter_custom_fusion.1
  56.2 116.2 %all-reduce.4.cloned.1.call-done = (f32[272,128]{1,0:T(8,128)}, f32[272,128]{1,0:T(8,128)}) async-done(((f32[272,128]{1,0:T(8,128)}, f32[272,128]{1,0:T(8,128)}), (f32[272,128]{1,0:T(8,128)}, f32[272,128]{1,0:T(8,128)})) %all-reduce.4.cloned.1.call-update) | async-done | bytes 278544 | tf_op jit(solution)/shard_map/pmax | solution.py:59
  172.4 1.6 multiply_reduce_fusion.4
  174.0 0.6 gather_fusion.2
  174.7 0.6 gather_fusion.4
  175.5 9.4 %fusion.6 = f32[128,1,128]{2,1,0:T(1,128)S(1)} fusion(f32[128,128,1]{1,2,0:T(1,128)S(1)} %bitcast.131, f32[1,1,128,128,128]{4,3,2,1,0:T(8,128)} %param.14), kind=kOutput, calls=%fused_computation.18 | convolution fusion | flops 25165824 | bytes 8519680 | tf_op jit(solution)/shard_map/tij,ti->tj/dot_general | solution.py:79
  184.9 5.6 %multiply_reduce_fusion.1 = f32[128,128]{1,0:T(8,128)S(1)} fusion(f32[1,1,128,128,128]{4,3,2,1,0:T(8,128)} %param.14, f32[128,128]{1,0:T(8,128)S(1)} %get-tuple-element.28, f32[128]{0:T(128)S(1)} %compare_convert_fusion), kind=kLoop, calls=%fused_computation.23 | loop fusion | flops 8372224 | bytes 8520192 | tf_op jit(solution)/shard_map/reduce_max | solution.py:55
  190.5 1.0 scatter_custom_fusion.2
  191.5 23.2 %pmax.30 = f32[64,128]{1,0:T(8,128)S(1)} all-reduce(f32[64,128]{1,0:T(8,128)S(1)} %scatter_custom_fusion.2), channel_id=1, replica_groups=mesh['row'=8,'col'=32] {'row'}, use_global_device_ids=true, to_apply=%region_8.11 | all-reduce | flops 8192 | bytes 65536 | tf_op jit(solution)/shard_map/pmax | solution.py:61
  214.7 0.6 multiply_reduce_fusion.5
  215.3 70.8 %psum.28 = f32[]{:T(128)} all-reduce(f32[]{:T(128)} %get-tuple-element.10), channel_id=1, replica_groups=mesh['row'=8,'col'=32] {'col'}, use_global_device_ids=true, to_apply=%region_10.13 | all-reduce | flops 1 | bytes 8 | tf_op jit(solution)/shard_map/psum | solution.py:72
  286.9 0.2 fusion.27
  287.1 21.8 %all-reduce.1 = (f32[64,128]{1,0:T(8,128)S(1)}, f32[]{:T(128)}) all-reduce(f32[64,128]{1,0:T(8,128)S(1)} %fusion.27, f32[]{:T(128)} %get-tuple-element.12), channel_id=1, replica_groups=mesh['row'=8,'col'=32] {'row'}, use_global_device_ids=true, to_apply=%region_16.19 | all-reduce | flops 8193 | bytes 65544 | tf_op jit(solution)/shard_map/psum | solution.py:80
  309.6 0.6 gather_fusion.5
  310.4 15.4 %fusion.4 = f32[128,1,128]{2,1,0:T(1,128)S(1)} fusion(f32[128,128,1]{1,2,0:T(1,128)S(1)} %bitcast.130, f32[1,1,128,128,128]{4,3,2,1,0:T(8,128)} %param.14), kind=kOutput, calls=%fused_computation.16 | convolution fusion | flops 25165824 | bytes 8519680 | tf_op jit(solution)/shard_map/tij,tj->ti/dot_general | solution.py:84
  325.8 0.3 fusion.11
  326.0 7.5 %collective-permute-start = (f32[272,128]{1,0:T(8,128)S(1)}, f32[272,128]{1,0:T(8,128)S(1)}, u32[]{:S(2)}, u32[]{:S(2)}) collective-permute-start(f32[272,128]{1,0:T(8,128)S(1)} %fusion.11), channel_id=1, source_target_pairs={{0,1},{1,0},{2,3},{3,2},{4,5},{5,4},{6,7},{7,6},{8,9},{9,8},{10,11... | collective-permute-start | bytes 417800 | tf_op jit(solution)/shard_map/ppermute | solution.py:16
  333.6 1.0 collective-permute-done
  334.7 4.9 %collective-permute-done.1 = f32[272,128]{1,0:T(8,128)S(1)} collective-permute-done((f32[272,128]{1,0:T(8,128)S(1)}, f32[272,128]{1,0:T(8,128)S(1)}, u32[]{:S(2)}, u32[]{:S(2)}) %collective-permute-start.1) | collective-permute-done | bytes 139296 | tf_op jit(solution)/shard_map/ppermute | solution.py:16
  339.7 5.4 %collective-permute-done.2 = f32[272,128]{1,0:T(8,128)S(1)} collective-permute-done((f32[272,128]{1,0:T(8,128)S(1)}, f32[272,128]{1,0:T(8,128)S(1)}, u32[]{:S(2)}, u32[]{:S(2)}) %collective-permute-start.2) | collective-permute-done | bytes 139296 | tf_op jit(solution)/shard_map/ppermute | solution.py:16
  345.2 3.9 collective-permute-done.3
  349.1 0.3 collective-permute-start.4
  349.4 5.4 %collective-permute-done.4 = f32[272,128]{1,0:T(8,128)S(1)} collective-permute-done((f32[272,128]{1,0:T(8,128)S(1)}, f32[272,128]{1,0:T(8,128)S(1)}, u32[]{:S(2)}, u32[]{:S(2)}) %collective-permute-start.4) | collective-permute-done | bytes 139296 | tf_op jit(solution)/shard_map/ppermute | solution.py:16
  354.9 0.6 gather_fusion.6
  355.6 9.4 %fusion.2 = f32[128,1,128]{2,1,0:T(1,128)S(1)} fusion(f32[128,128,1]{1,2,0:T(1,128)S(1)} %bitcast.127, f32[1,1,128,128,128]{4,3,2,1,0:T(8,128)} %param.14), kind=kOutput, calls=%fused_computation.14 | convolution fusion | flops 25165824 | bytes 8519680 | tf_op jit(solution)/shard_map/tij,ti->tj/dot_general | solution.py:79
  365.0 0.2 fusion.25
  365.2 21.6 %psum.31 = f32[64,128]{1,0:T(8,128)S(1)} all-reduce(f32[64,128]{1,0:T(8,128)S(1)} %fusion.25), channel_id=1, replica_groups=mesh['row'=8,'col'=32] {'row'}, use_global_device_ids=true, to_apply=%region_17.20 | all-reduce | flops 8192 | bytes 65536 | tf_op jit(solution)/shard_map/psum | solution.py:80
  386.8 0.6 subtract_multiply_fusion
  387.5 0.6 gather_fusion.7
  388.2 15.4 %fusion = f32[128,1,128]{2,1,0:T(1,128)S(1)} fusion(f32[128,128,1]{1,2,0:T(1,128)S(1)} %bitcast.129, f32[1,1,128,128,128]{4,3,2,1,0:T(8,128)} %param.14), kind=kOutput, calls=%fused_computation.12 | convolution fusion | flops 25165824 | bytes 8519680 | tf_op jit(solution)/shard_map/tij,tj->ti/dot_general | solution.py:84
  403.6 0.3 fusion.9
  403.9 13.3 %collective-permute-start.5 = (f32[272,128]{1,0:T(8,128)S(1)}, f32[272,128]{1,0:T(8,128)S(1)}, u32[]{:S(2)}, u32[]{:S(2)}) collective-permute-start(f32[272,128]{1,0:T(8,128)S(1)} %fusion.9), channel_id=1, source_target_pairs={{0,1},{1,0},{2,3},{3,2},{4,5},{5,4},{6,7},{7,6},{8,9},{9,8},{10,11... | collective-permute-start | bytes 417800 | tf_op jit(solution)/shard_map/ppermute | solution.py:16
  417.2 1.0 collective-permute-done.5
  418.3 4.9 %collective-permute-done.6 = f32[272,128]{1,0:T(8,128)S(1)} collective-permute-done((f32[272,128]{1,0:T(8,128)S(1)}, f32[272,128]{1,0:T(8,128)S(1)}, u32[]{:S(2)}, u32[]{:S(2)}) %collective-permute-start.6) | collective-permute-done | bytes 139296 | tf_op jit(solution)/shard_map/ppermute | solution.py:16
  423.3 5.4 %collective-permute-done.7 = f32[272,128]{1,0:T(8,128)S(1)} collective-permute-done((f32[272,128]{1,0:T(8,128)S(1)}, f32[272,128]{1,0:T(8,128)S(1)}, u32[]{:S(2)}, u32[]{:S(2)}) %collective-permute-start.7) | collective-permute-done | bytes 139296 | tf_op jit(solution)/shard_map/ppermute | solution.py:16
  428.8 3.9 collective-permute-done.8
  432.8 5.4 %collective-permute-done.9 = f32[272,128]{1,0:T(8,128)S(1)} collective-permute-done((f32[272,128]{1,0:T(8,128)S(1)}, f32[272,128]{1,0:T(8,128)S(1)}, u32[]{:S(2)}, u32[]{:S(2)}) %collective-permute-start.9) | collective-permute-done | bytes 139296 | tf_op jit(solution)/shard_map/ppermute | solution.py:16
  438.2 0.8 multiply_bitcast_fusion
  (44 shorter events, 1.5 us)
Async XLA Ops:
  7.2 165.2 %all-reduce.4.cloned.1.call-start = ((), (), s32[]{:S(2)}) async-start(), calls=%async_computation | async-start | bytes 557056 | tf_op jit(solution)/shard_map/pmax | solution.py:59
  10.2 162.2 %copy-start = (f32[34816]{0:T(1024)S(1)}, f32[34816]{0:T(1024)}, u32[]{:S(2)}) copy-start(f32[34816]{0:T(1024)} %param.20) | copy-start | bytes 417796
  10.2 164.4 %copy-start.1 = (f32[34816]{0:T(1024)S(1)}, f32[34816]{0:T(1024)}, u32[]{:S(2)}) copy-start(f32[34816]{0:T(1024)} %param.22) | copy-start | bytes 417796
  175.4 39.3 %copy-start.2 = (f32[8192]{0:T(1024)S(1)}, f32[8192]{0:T(1024)}, u32[]{:S(2)}) copy-start(f32[8192]{0:T(1024)} %param.17) | copy-start | bytes 98308
  175.4 134.2 %copy-start.3 = (f32[8192]{0:T(1024)S(1)}, f32[8192]{0:T(1024)}, u32[]{:S(2)}) copy-start(f32[8192]{0:T(1024)} %param.19) | copy-start | bytes 98308
  175.4 134.2 %copy-start.4 = (f32[8192]{0:T(1024)S(1)}, f32[8192]{0:T(1024)}, u32[]{:S(2)}) copy-start(f32[8192]{0:T(1024)} %param.18) | copy-start | bytes 98308
  175.4 134.2 %copy-start.5 = (f32[8192]{0:T(1024)S(1)}, f32[8192]{0:T(1024)}, u32[]{:S(2)}) copy-start(f32[8192]{0:T(1024)} %param.21) | copy-start | bytes 98308
  326.0 8.5 %collective-permute-start = (f32[272,128]{1,0:T(8,128)S(1)}, f32[272,128]{1,0:T(8,128)S(1)}, u32[]{:S(2)}, u32[]{:S(2)}) collective-permute-start(f32[272,128]{1,0:T(8,128)S(1)} %fusion.11), channel_id=1, source_target_pairs={{0,1},{1,0},{2,3},{3,2},{4,5},{5,4},{6,7},{7,6},{8,9},{9,8},{10,11... | collective-permute-start | bytes 417800 | tf_op jit(solution)/shard_map/ppermute | solution.py:16
  334.6 5.0 %collective-permute-start.1 = (f32[272,128]{1,0:T(8,128)S(1)}, f32[272,128]{1,0:T(8,128)S(1)}, u32[]{:S(2)}, u32[]{:S(2)}) collective-permute-start(f32[272,128]{1,0:T(8,128)S(1)} %add.92), channel_id=1, source_target_pairs={{0,2},{1,3},{2,0},{3,1},{4,6},{5,7},{6,4},{7,5},{8,10},{9,11},{10,... | collective-permute-start | bytes 417800 | tf_op jit(solution)/shard_map/ppermute | solution.py:16
  339.6 5.5 %collective-permute-start.2 = (f32[272,128]{1,0:T(8,128)S(1)}, f32[272,128]{1,0:T(8,128)S(1)}, u32[]{:S(2)}, u32[]{:S(2)}) collective-permute-start(f32[272,128]{1,0:T(8,128)S(1)} %add.93), channel_id=1, source_target_pairs={{0,4},{1,5},{2,6},{3,7},{4,0},{5,1},{6,2},{7,3},{8,12},{9,13},{10,... | collective-permute-start | bytes 417800 | tf_op jit(solution)/shard_map/ppermute | solution.py:16
  345.1 4.0 collective-permute-start.3
  349.1 5.7 %collective-permute-start.4 = (f32[272,128]{1,0:T(8,128)S(1)}, f32[272,128]{1,0:T(8,128)S(1)}, u32[]{:S(2)}, u32[]{:S(2)}) collective-permute-start(f32[272,128]{1,0:T(8,128)S(1)} %add.95), channel_id=1, source_target_pairs={{0,16},{1,17},{2,18},{3,19},{4,20},{5,21},{6,22},{7,23},{8,24},{9,... | collective-permute-start | bytes 417800 | tf_op jit(solution)/shard_map/ppermute | solution.py:16
  403.9 14.3 %collective-permute-start.5 = (f32[272,128]{1,0:T(8,128)S(1)}, f32[272,128]{1,0:T(8,128)S(1)}, u32[]{:S(2)}, u32[]{:S(2)}) collective-permute-start(f32[272,128]{1,0:T(8,128)S(1)} %fusion.9), channel_id=1, source_target_pairs={{0,1},{1,0},{2,3},{3,2},{4,5},{5,4},{6,7},{7,6},{8,9},{9,8},{10,11... | collective-permute-start | bytes 417800 | tf_op jit(solution)/shard_map/ppermute | solution.py:16
  418.2 5.0 %collective-permute-start.6 = (f32[272,128]{1,0:T(8,128)S(1)}, f32[272,128]{1,0:T(8,128)S(1)}, u32[]{:S(2)}, u32[]{:S(2)}) collective-permute-start(f32[272,128]{1,0:T(8,128)S(1)} %add.98), channel_id=1, source_target_pairs={{0,2},{1,3},{2,0},{3,1},{4,6},{5,7},{6,4},{7,5},{8,10},{9,11},{10,... | collective-permute-start | bytes 417800 | tf_op jit(solution)/shard_map/ppermute | solution.py:16
  423.2 5.5 %collective-permute-start.7 = (f32[272,128]{1,0:T(8,128)S(1)}, f32[272,128]{1,0:T(8,128)S(1)}, u32[]{:S(2)}, u32[]{:S(2)}) collective-permute-start(f32[272,128]{1,0:T(8,128)S(1)} %add.99), channel_id=1, source_target_pairs={{0,4},{1,5},{2,6},{3,7},{4,0},{5,1},{6,2},{7,3},{8,12},{9,13},{10,... | collective-permute-start | bytes 417800 | tf_op jit(solution)/shard_map/ppermute | solution.py:16
  428.7 4.0 collective-permute-start.8
  432.7 5.5 %collective-permute-start.9 = (f32[272,128]{1,0:T(8,128)S(1)}, f32[272,128]{1,0:T(8,128)S(1)}, u32[]{:S(2)}, u32[]{:S(2)}) collective-permute-start(f32[272,128]{1,0:T(8,128)S(1)} %add.101), channel_id=1, source_target_pairs={{0,16},{1,17},{2,18},{3,19},{4,20},{5,21},{6,22},{7,23},{8,24},{9,... | collective-permute-start | bytes 417800 | tf_op jit(solution)/shard_map/ppermute | solution.py:16
Sparse Core Ops, SparseCore 0:
  55.7 116.6 all-reduce.3
